TPU v7x, 32 devices: a whole 2x2x4 slice. The times are simulated.
32 devices in a mesh: ctx: 4 (over y, core), ep: 8 (over z, x).
Axes of the slice: x: 2, y: 2, z: 4, core: 2. Of those that a mesh axis runs over, the one named last changes fastest.
Arguments:
- tokens: bfloat16 [1024, 3584], P('ep', 'ctx'), may hold values from -6 to 6
- cotangent: bfloat16 [1024, 3584], P('ep', 'ctx'), may hold values from -0.8984375 to 0.8984375
- expert_ids: int32 [1024, 1], P('ep'), may hold values from 0 to 7; in each aligned block of 128 rows (0 to 127, 128 to 255, ...) at most 24 rows name the same one
- route_gates: float32 [1024, 1], P('ep'), may hold values from 0.1 to 1
- w_gate: bfloat16 [8, 3584, 2048], P('ep', None, 'ctx'), may hold values from -0.125 to 0.125
- w_up: bfloat16 [8, 3584, 2048], P('ep', None, 'ctx'), may hold values from -0.09375 to 0.09375
- w_down: bfloat16 [8, 2048, 3584], P('ep', 'ctx'), may hold values from -0.1875 to 0.1875
Outputs:
- layer_out: bfloat16 [1024, 3584], P('ep', 'ctx')
- input_grad: bfloat16 [1024, 3584], P('ep', 'ctx')
- gate_grad: float32 [1024, 1], P('ep')
- w_gate_grad: bfloat16 [8, 3584, 2048], P('ep', None, 'ctx')
- w_up_grad: bfloat16 [8, 3584, 2048], P('ep', None, 'ctx')
Inputs may be any that keep to these rules, and one draw needn't show every extreme that they name: `expert_ids`: within each aligned block of 128 tokens (the tokens of one index of ep) no expert is named more than 24 times, a bound that some block reaches; the routes of one token name different experts.
All inputs are finite; a program needn't handle non-finite values.
Results may differ from a plain program's by a relative error of at most 0.015.
Values may be sent and summed in bfloat16 or wider, within the bound.
No kernel may reach another device: no remote copies, remote signals or barrier semaphores. Data moves between devices by JAX's collectives and lax.ppermute only.
A program may use at most 128 MiB of HBM per device.

v0:
```python
import jax
import jax.numpy as jnp
from jax import lax
from jax.sharding import PartitionSpec as P


def route_onehot(expert_ids, experts, capacity):
    tok_rows, routes = expert_ids.shape
    flat_ids = expert_ids.reshape(-1)
    labels = jnp.arange(experts, dtype=jnp.int32)
    onehot = (flat_ids[:, None] == labels[None, :]).astype(jnp.bfloat16)
    pairs = jnp.arange(flat_ids.shape[0], dtype=jnp.int32)
    before = (pairs[:, None] > pairs[None, :]).astype(jnp.bfloat16)
    earlier = jnp.dot(before, onehot, preferred_element_type=jnp.float32)
    slot_rank = jnp.sum(earlier * onehot.astype(jnp.float32), axis=1).astype(jnp.int32)
    slot_ids = (flat_ids * capacity + slot_rank).reshape(tok_rows, routes)
    positions = jnp.arange(experts * capacity, dtype=jnp.int32)
    return [slot_ids[:, r][:, None] == positions[None, :] for r in range(routes)]


def split_f32(values):
    hi = values.astype(jnp.bfloat16)
    lo = (values - hi.astype(jnp.float32)).astype(jnp.bfloat16)
    return (hi, lo)


def join_f32(hi, lo):
    return hi.astype(jnp.float32) + lo.astype(jnp.float32)


def ctx_bits(n_ctx):
    bits = n_ctx.bit_length() - 1
    assert 1 << bits == n_ctx
    return bits


def xor_pairs(n_ctx, bit):
    return [(i, i ^ 1 << bit) for i in range(n_ctx)]


def gather_blocks(block, n_ctx, me):
    held = block[None]
    for bit in reversed(range(ctx_bits(n_ctx))):
        other = lax.ppermute(held, "ctx", xor_pairs(n_ctx, bit))
        mine_first = me >> bit & 1 == 0
        pair = jnp.where(
            mine_first, jnp.stack([held, other], axis=1), jnp.stack([other, held], axis=1)
        )
        held = pair.reshape((-1,) + block.shape)
    return held


def scatter_sum(blocks, n_ctx, me):
    acc = blocks
    for bit in range(ctx_bits(n_ctx)):
        halves = acc.reshape((-1, 2) + acc.shape[1:])
        keep_first = me >> bit & 1 == 0
        keep = jnp.where(keep_first, halves[:, 0], halves[:, 1])
        send = jnp.where(keep_first, halves[:, 1], halves[:, 0]).astype(jnp.bfloat16)
        got = lax.ppermute(send, "ctx", xor_pairs(n_ctx, bit))
        acc = keep + got.astype(jnp.float32)
    return acc[0]


def all_sum(values, n_ctx):
    for bit in range(ctx_bits(n_ctx)):
        values = values + lax.ppermute(values, "ctx", xor_pairs(n_ctx, bit))
    return values


def with_cols(rows, values, pad):
    hi, lo = split_f32(values)
    zeros = jnp.zeros((rows.shape[0], pad - 2), jnp.bfloat16)
    return jnp.concatenate([rows, hi[:, None], lo[:, None], zeros], axis=1)


def shards(tokens, cotangent, expert_ids, route_gates, w_gate, w_up, w_down):
    tok_rows, routes = expert_ids.shape
    experts = lax.axis_size("ep")
    n_ctx = lax.axis_size("ctx")
    me = lax.axis_index("ctx")
    capacity = 3 * tok_rows * routes // (2 * experts)
    slot_count = experts * capacity
    col_width = tokens.shape[1]
    pad = 128
    route_maps = route_onehot(expert_ids, experts, capacity)

    def place(values):
        placed = jnp.zeros((slot_count, values.shape[1]), jnp.float32)
        for chosen in route_maps:
            placed = placed + jnp.einsum(
                "ts,tc->sc", chosen.astype(jnp.bfloat16), values, preferred_element_type=jnp.float32
            )
        return placed.astype(jnp.bfloat16)

    def to_experts(rows):
        sent = rows.reshape(experts, capacity, rows.shape[1])
        got = lax.all_to_all(sent, "ep", split_axis=0, concat_axis=0, tiled=True)
        return got.reshape(slot_count, rows.shape[1])

    slot_gates = jnp.zeros((slot_count,), jnp.float32)
    for r, chosen in enumerate(route_maps):
        slot_gates = slot_gates + jnp.sum(
            jnp.where(chosen, route_gates[:, r][:, None], 0.0), axis=0
        )
    got_x = to_experts(with_cols(place(tokens), slot_gates, pad))
    gate_column = join_f32(got_x[:, col_width], got_x[:, col_width + 1])[:, None]
    rows_in = gather_blocks(got_x[:, :col_width], n_ctx, me)
    got_dy = to_experts(place(cotangent))
    grads_in = gather_blocks(got_dy, n_ctx, me)
    group = w_gate.shape[2]
    gate_w = w_gate[0].reshape(n_ctx, col_width, group)
    up_w = w_up[0].reshape(n_ctx, col_width, group)
    down_w = w_down[0]
    down_cols = [down_w[:, q * col_width : (q + 1) * col_width] for q in range(n_ctx)]
    pre_gate = jnp.einsum("nsd,ndf->sf", rows_in, gate_w, preferred_element_type=jnp.float32)
    pre_up = jnp.einsum("nsd,ndf->sf", rows_in, up_w, preferred_element_type=jnp.float32)
    sigma = jax.nn.sigmoid(pre_gate)
    activated = pre_gate * sigma
    hidden = (activated * pre_up).astype(jnp.bfloat16)
    partial_out = jnp.stack(
        [jnp.dot(hidden, cols, preferred_element_type=jnp.float32) for cols in down_cols]
    ).astype(jnp.bfloat16)
    gate_part = jnp.einsum(
        "nsd,nsd->s", partial_out.astype(jnp.float32), grads_in.astype(jnp.float32)
    )
    expert_out = scatter_sum(partial_out.astype(jnp.float32), n_ctx, me).astype(jnp.bfloat16)
    gate_sum = all_sum(gate_part, n_ctx)
    back_out = to_experts(with_cols(expert_out, gate_sum, pad))
    contract_last = (((1,), (1,)), ((), ()))
    down_t = sum(
        (
            lax.dot_general(
                grads_in[q], down_cols[q], contract_last, preferred_element_type=jnp.float32
            )
            for q in range(n_ctx)
        )
    )
    hidden_grad = gate_column * down_t
    grad_gate = (hidden_grad * pre_up * sigma * (1.0 + pre_gate * (1.0 - sigma))).astype(
        jnp.bfloat16
    )
    grad_up = (hidden_grad * activated).astype(jnp.bfloat16)
    back_terms = jnp.einsum(
        "sf,ndf->nsd", grad_gate, gate_w, preferred_element_type=jnp.float32
    ) + jnp.einsum("sf,ndf->nsd", grad_up, up_w, preferred_element_type=jnp.float32)
    back_terms = back_terms.astype(jnp.bfloat16).astype(jnp.float32)
    slot_grad = scatter_sum(back_terms, n_ctx, me).astype(jnp.bfloat16)
    back_grad = to_experts(slot_grad)
    w_gate_grad = (
        jnp.einsum("nsd,sf->ndf", rows_in, grad_gate, preferred_element_type=jnp.float32)
        .astype(jnp.bfloat16)
        .reshape(1, n_ctx * col_width, group)
    )
    w_up_grad = (
        jnp.einsum("nsd,sf->ndf", rows_in, grad_up, preferred_element_type=jnp.float32)
        .astype(jnp.bfloat16)
        .reshape(1, n_ctx * col_width, group)
    )
    layer_out = jnp.zeros((tok_rows, col_width), jnp.float32)
    input_grad = jnp.zeros((tok_rows, col_width), jnp.float32)
    gate_terms = []
    for r, chosen in enumerate(route_maps):
        pick = chosen.astype(jnp.bfloat16)
        rows_r = jnp.dot(pick, back_out, preferred_element_type=jnp.float32)
        layer_out = layer_out + route_gates[:, r][:, None] * rows_r[:, :col_width]
        input_grad = input_grad + jnp.dot(pick, back_grad, preferred_element_type=jnp.float32)
        gate_terms.append(rows_r[:, col_width] + rows_r[:, col_width + 1])
    gate_grad = jnp.stack(gate_terms, axis=1)
    return (
        layer_out.astype(jnp.bfloat16),
        input_grad.astype(jnp.bfloat16),
        gate_grad,
        w_gate_grad,
        w_up_grad,
    )


def solution(mesh):
    in_specs = (
        P("ep", "ctx"),
        P("ep", "ctx"),
        P("ep", None),
        P("ep", None),
        P("ep", None, "ctx"),
        P("ep", None, "ctx"),
        P("ep", "ctx", None),
    )
    out_specs = (
        P("ep", "ctx"),
        P("ep", "ctx"),
        P("ep", None),
        P("ep", None, "ctx"),
        P("ep", None, "ctx"),
    )
    return jax.shard_map(shards, mesh=mesh, in_specs=in_specs, out_specs=out_specs, check_vma=False)
```

profile of v0, /device:TPU:0, one launch (start us, length us, event | category | flops | bytes accessed | tf_op | source)
XLA Modules:
  0.0 105.1 jit_solution(2697727353516576229)
XLA Ops:
  0.7 0.9 fusion.7
  2.2 1.0 convolution_convert_fusion.2
  3.2 7.3 %all-to-all-start.1 = ((bf16[8,24,896]{2,1,0:T(8,128)(2,1)}), bf16[8,24,896]{2,1,0:T(8,128)(2,1)S(1)}, u32[]{:S(2)}, u32[]{:S(2)}) async-start(bf16[8,24,896]{2,1,0:T(8,128)(2,1)} %bitcast.34), calls=%async_computation.1 | async-start | bytes 688128 | tf_op jit(solution)/shard_map/all_to_all | solution.py:98
  12.8 8.3 %all-to-all-done.1 = bf16[8,24,896]{2,1,0:T(8,128)(2,1)S(1)} async-done(((bf16[8,24,896]{2,1,0:T(8,128)(2,1)}), bf16[8,24,896]{2,1,0:T(8,128)(2,1)S(1)}, u32[]{:S(2)}, u32[]{:S(2)}) %all-to-all-start.1) | async-done | bytes 344096 | tf_op jit(solution)/shard_map/all_to_all | solution.py:98
  21.1 3.6 %all-to-all-start = ((bf16[8,24,1024]{2,1,0:T(8,128)(2,1)}), bf16[8,24,1024]{2,1,0:T(8,128)(2,1)S(1)}, u32[]{:S(2)}, u32[]{:S(2)}) async-start(bf16[8,24,1024]{2,1,0:T(8,128)(2,1)} %maximum_maximum_fusion), calls=%async_computation | async-start | bytes 786432 | tf_op jit(solution)/shard_map/all_to_all | solution.py:98
  24.7 1.5 %collective-permute-start.4 = (bf16[1,192,896]{2,1,0:T(8,128)(2,1)S(1)}, bf16[1,192,896]{2,1,0:T(8,128)(2,1)S(1)}, u32[]{:S(2)}, u32[]{:S(2)}) collective-permute-start(bf16[1,192,896]{2,1,0:T(8,128)(2,1)S(1)} %bitcast.174), channel_id=1, source_target_pairs={{0,16},{8,24},{16,0},{24,8},{1,17},{9,25},{17,1},{25,9},{2,18},{10... | collective-permute-start | bytes 1032200 | tf_op jit(solution)/shard_map/ppermute | solution.py:44
  26.2 7.5 %collective-permute-done.4 = bf16[1,192,896]{2,1,0:T(8,128)(2,1)S(1)} collective-permute-done((bf16[1,192,896]{2,1,0:T(8,128)(2,1)S(1)}, bf16[1,192,896]{2,1,0:T(8,128)(2,1)S(1)}, u32[]{:S(2)}, u32[]{:S(2)}) %collective-permute-start.4) | collective-permute-done | bytes 344096 | tf_op jit(solution)/shard_map/ppermute | solution.py:44
  33.8 1.0 maximum_select_fusion.4
  34.7 1.2 %all-to-all-done = bf16[8,24,1024]{2,1,0:T(8,128)(2,1)S(1)} async-done(((bf16[8,24,1024]{2,1,0:T(8,128)(2,1)}), bf16[8,24,1024]{2,1,0:T(8,128)(2,1)S(1)}, u32[]{:S(2)}, u32[]{:S(2)}) %all-to-all-start) | async-done | bytes 393248 | tf_op jit(solution)/shard_map/all_to_all | solution.py:98
  36.0 1.6 %collective-permute-start = (bf16[1,192,896]{2,1,0:T(8,128)(2,1)S(1)}, bf16[1,192,896]{2,1,0:T(8,128)(2,1)S(1)}, u32[]{:S(2)}, u32[]{:S(2)}) collective-permute-start(bf16[1,192,896]{2,1,0:T(8,128)(2,1)S(1)} %get-tuple-element.33), channel_id=1, source_target_pairs={{0,16},{8,24},{16,0},{24,8},{1,17},{9,25},{17,1},{25,9},{2,18},{10... | collective-permute-start | bytes 1032200 | tf_op jit(solution)/shard_map/ppermute | solution.py:44
  37.9 7.4 %collective-permute-done = bf16[1,192,896]{2,1,0:T(8,128)(2,1)S(1)} collective-permute-done((bf16[1,192,896]{2,1,0:T(8,128)(2,1)S(1)}, bf16[1,192,896]{2,1,0:T(8,128)(2,1)S(1)}, u32[]{:S(2)}, u32[]{:S(2)}) %collective-permute-start) | collective-permute-done | bytes 344096 | tf_op jit(solution)/shard_map/ppermute | solution.py:44
  46.1 1.6 %copy-done.3 = bf16[1,512,3584]{2,1,0:T(8,128)(2,1)S(1)} copy-done((bf16[1,512,3584]{2,1,0:T(8,128)(2,1)S(1)}, bf16[1,512,3584]{2,1,0:T(8,128)(2,1)}, u32[]{:S(2)}) %copy-start.3) | copy-done | bytes 3670040
  49.4 1.3 %copy-done.2 = bf16[1,3584,512]{2,1,0:T(8,128)(2,1)S(1)} copy-done((bf16[1,3584,512]{2,1,0:T(8,128)(2,1)S(1)}, bf16[1,3584,512]{2,1,0:T(8,128)(2,1)}, u32[]{:S(2)}) %copy-start.2) | copy-done | bytes 3670040
  50.7 0.9 convolution_bitcast_fusion.4
  51.6 1.2 %copy-done.1 = bf16[1,3584,512]{2,1,0:T(8,128)(2,1)S(1)} copy-done((bf16[1,3584,512]{2,1,0:T(8,128)(2,1)S(1)}, bf16[1,3584,512]{2,1,0:T(8,128)(2,1)}, u32[]{:S(2)}) %copy-start.1) | copy-done | bytes 3670040
  52.7 0.9 convolution_bitcast_fusion.5
  55.7 1.3 %fusion.27 = f32[192,4,896]{2,0,1:T(8,128)S(1)} fusion(bf16[4,896,512]{2,1,0:T(8,128)(2,1)S(1)} %bitcast.169, bf16[192,512]{1,0:T(8,128)(2,1)S(1)} %get-tuple-element.30), kind=kOutput, calls=%fused_computation.74 | convolution fusion | flops 704643072 | bytes 6619136 | tf_op jit(solution)/shard_map/sf,ndf->nsd/dot_general | solution.py:144
  57.1 1.3 %fusion.1 = f32[192,4,896]{2,0,1:T(8,128)S(1)} fusion(f32[192,4,896]{2,0,1:T(8,128)S(1)} %fusion.27, bf16[192,512,1]{1,0,2:T(8,128)(2,1)S(1)} %get-tuple-element.29, bf16[4,896,512]{2,1,0:T(8,128)(2,1)S(1)} %bitcast.171), kind=kOutput, calls=%fused_computation.6 | convolution fusion | flops 706707456 | bytes 9371648 | tf_op jit(solution)/shard_map/sf,ndf->nsd/dot_general | solution.py:146
  60.5 1.6 %collective-permute-done.6 = f32[192]{0:T(256)S(1)} collective-permute-done((f32[192]{0:T(256)S(1)}, f32[192]{0:T(256)S(1)}, u32[]{:S(2)}, u32[]{:S(2)}) %collective-permute-start.6) | collective-permute-done | bytes 800 | tf_op jit(solution)/shard_map/ppermute | solution.py:67
  62.2 1.5 %collective-permute-start.7 = (f32[192]{0:T(256)S(1)}, f32[192]{0:T(256)S(1)}, u32[]{:S(2)}, u32[]{:S(2)}) collective-permute-start(f32[192]{0:T(256)S(1)} %add.53), channel_id=1, source_target_pairs={{0,16},{8,24},{16,0},{24,8},{1,17},{9,25},{17,1},{25,9},{2,18},{10... | collective-permute-start | bytes 2312 | tf_op jit(solution)/shard_map/ppermute | solution.py:67
  65.5 1.5 %collective-permute-start.3 = (bf16[1,192,896]{2,1,0:T(8,128)(2,1)}, bf16[1,192,896]{2,1,0:T(8,128)(2,1)}, u32[]{:S(2)}, u32[]{:S(2)}) collective-permute-start(bf16[1,192,896]{2,1,0:T(8,128)(2,1)} %fusion.23), channel_id=1, source_target_pairs={{0,16},{8,24},{16,0},{24,8},{1,17},{9,25},{17,1},{25,9},{2,18},{10... | collective-permute-start | bytes 1032200 | tf_op jit(solution)/shard_map/ppermute | solution.py:60
  67.0 7.9 %collective-permute-done.9 = bf16[1,192,896]{2,1,0:T(8,128)(2,1)S(1)} collective-permute-done((bf16[1,192,896]{2,1,0:T(8,128)(2,1)S(1)}, bf16[1,192,896]{2,1,0:T(8,128)(2,1)S(1)}, u32[]{:S(2)}, u32[]{:S(2)}) %collective-permute-start.9) | collective-permute-done | bytes 344096 | tf_op jit(solution)/shard_map/ppermute | solution.py:60
  75.8 5.7 %all-to-all-start.3 = ((bf16[8,24,896]{2,1,0:T(8,128)(2,1)}), bf16[8,24,896]{2,1,0:T(8,128)(2,1)S(1)}, u32[]{:S(2)}, u32[]{:S(2)}) async-start(bf16[8,24,896]{2,1,0:T(8,128)(2,1)} %bitcast.185), calls=%async_computation.3 | async-start | bytes 688128 | tf_op jit(solution)/shard_map/all_to_all | solution.py:98
  81.5 0.9 concatenate.62
  82.4 0.9 concatenate.63
  83.2 1.1 %fusion.20 = bf16[1,192,896]{2,1,0:T(8,128)(2,1)S(1)} fusion(bf16[1,192,896]{2,1,0:T(8,128)(2,1)} %collective-permute-done.3, f32[1,2,192,896]{3,2,1,0:T(8,128)S(1)} %fusion.4, pred[]{:T(512)S(6)} %eq.50), kind=kLoop, calls=%fused_computation.52 | loop fusion | flops 688128 | bytes 2064385 | tf_op jit(solution)/shard_map/convert_element_type | solution.py:127
  85.2 5.2 %all-to-all-done.3 = bf16[8,24,896]{2,1,0:T(8,128)(2,1)S(1)} async-done(((bf16[8,24,896]{2,1,0:T(8,128)(2,1)}), bf16[8,24,896]{2,1,0:T(8,128)(2,1)S(1)}, u32[]{:S(2)}, u32[]{:S(2)}) %all-to-all-start.3) | async-done | bytes 344096 | tf_op jit(solution)/shard_map/all_to_all | solution.py:98
  90.3 3.6 %all-to-all-start.2 = ((bf16[8,24,1024]{2,1,0:T(8,128)(2,1)}), bf16[8,24,1024]{2,1,0:T(8,128)(2,1)S(1)}, u32[]{:S(2)}, u32[]{:S(2)}) async-start(bf16[8,24,1024]{2,1,0:T(8,128)(2,1)} %maximum_maximum_fusion.1), calls=%async_computation.2 | async-start | bytes 786432 | tf_op jit(solution)/shard_map/all_to_all | solution.py:98
  94.0 3.0 %convolution_convert_fusion = bf16[4,896,512]{2,1,0:T(8,128)(2,1)} fusion(bf16[4,192,896]{2,1,0:T(8,128)(2,1)S(1)} %bitcast.160, bf16[192,512,1]{1,0,2:T(8,128)(2,1)S(1)} %copy-done.5), kind=kOutput, calls=%fused_computation.4 | convolution fusion | flops 706478080 | bytes 5242880 | tf_op jit(solution)/shard_map/nsd,sf->ndf/dot_general | solution.py:156
  97.0 3.0 %convolution_convert_fusion.1 = bf16[4,896,512]{2,1,0:T(8,128)(2,1)} fusion(bf16[4,192,896]{2,1,0:T(8,128)(2,1)S(1)} %bitcast.161, bf16[192,512]{1,0:T(8,128)(2,1)S(1)} %get-tuple-element.30), kind=kOutput, calls=%fused_computation.5 | convolution fusion | flops 706478080 | bytes 5242880 | tf_op jit(solution)/shard_map/nsd,sf->ndf/dot_general | solution.py:151
  100.0 1.0 convolution_convert_fusion.4
  101.0 2.4 %all-to-all-done.2 = bf16[8,24,1024]{2,1,0:T(8,128)(2,1)S(1)} async-done(((bf16[8,24,1024]{2,1,0:T(8,128)(2,1)}), bf16[8,24,1024]{2,1,0:T(8,128)(2,1)S(1)}, u32[]{:S(2)}, u32[]{:S(2)}) %all-to-all-start.2) | async-done | bytes 393248 | tf_op jit(solution)/shard_map/all_to_all | solution.py:98
  (71 shorter events, 15.0 us)
Async XLA Ops:
  0.6 1.6 %copy-start = (bf16[128,896]{1,0:T(8,128)(2,1)S(1)}, bf16[128,896]{1,0:T(8,128)(2,1)}, u32[]{:S(2)}) copy-start(bf16[128,896]{1,0:T(8,128)(2,1)} %param.8) | copy-start | bytes 688132
  0.6 11.0 %copy-start.6 = (bf16[128,896]{1,0:T(8,128)(2,1)S(1)}, bf16[128,896]{1,0:T(8,128)(2,1)}, u32[]{:S(2)}) copy-start(bf16[128,896]{1,0:T(8,128)(2,1)} %param.7) | copy-start | bytes 688132
  3.2 17.9 %all-to-all-start.1 = ((bf16[8,24,896]{2,1,0:T(8,128)(2,1)}), bf16[8,24,896]{2,1,0:T(8,128)(2,1)S(1)}, u32[]{:S(2)}, u32[]{:S(2)}) async-start(bf16[8,24,896]{2,1,0:T(8,128)(2,1)} %bitcast.34), calls=%async_computation.1 | async-start | bytes 688128 | tf_op jit(solution)/shard_map/all_to_all | solution.py:98
  21.1 14.9 %all-to-all-start = ((bf16[8,24,1024]{2,1,0:T(8,128)(2,1)}), bf16[8,24,1024]{2,1,0:T(8,128)(2,1)S(1)}, u32[]{:S(2)}, u32[]{:S(2)}) async-start(bf16[8,24,1024]{2,1,0:T(8,128)(2,1)} %maximum_maximum_fusion), calls=%async_computation | async-start | bytes 786432 | tf_op jit(solution)/shard_map/all_to_all | solution.py:98
  24.7 9.1 %collective-permute-start.4 = (bf16[1,192,896]{2,1,0:T(8,128)(2,1)S(1)}, bf16[1,192,896]{2,1,0:T(8,128)(2,1)S(1)}, u32[]{:S(2)}, u32[]{:S(2)}) collective-permute-start(bf16[1,192,896]{2,1,0:T(8,128)(2,1)S(1)} %bitcast.174), channel_id=1, source_target_pairs={{0,16},{8,24},{16,0},{24,8},{1,17},{9,25},{17,1},{25,9},{2,18},{10... | collective-permute-start | bytes 1032200 | tf_op jit(solution)/shard_map/ppermute | solution.py:44
  34.7 10.9 %collective-permute-start.5 = (bf16[2,192,896]{2,1,0:T(8,128)(2,1)}, bf16[2,192,896]{2,1,0:T(8,128)(2,1)S(1)}, u32[]{:S(2)}, u32[]{:S(2)}) collective-permute-start(bf16[2,192,896]{2,1,0:T(8,128)(2,1)} %maximum_select_fusion.4), channel_id=1, source_target_pairs={{0,8},{8,0},{16,24},{24,16},{1,9},{9,1},{17,25},{25,17},{2,10},{10... | collective-permute-start | bytes 2064392 | tf_op jit(solution)/shard_map/ppermute | solution.py:44
  36.0 9.3 %collective-permute-start = (bf16[1,192,896]{2,1,0:T(8,128)(2,1)S(1)}, bf16[1,192,896]{2,1,0:T(8,128)(2,1)S(1)}, u32[]{:S(2)}, u32[]{:S(2)}) collective-permute-start(bf16[1,192,896]{2,1,0:T(8,128)(2,1)S(1)} %get-tuple-element.33), channel_id=1, source_target_pairs={{0,16},{8,24},{16,0},{24,8},{1,17},{9,25},{17,1},{25,9},{2,18},{10... | collective-permute-start | bytes 1032200 | tf_op jit(solution)/shard_map/ppermute | solution.py:44
  45.5 3.7 %collective-permute-start.1 = (bf16[2,192,896]{2,1,0:T(8,128)(2,1)S(1)}, bf16[2,192,896]{2,1,0:T(8,128)(2,1)S(1)}, u32[]{:S(2)}, u32[]{:S(2)}) collective-permute-start(bf16[2,192,896]{2,1,0:T(8,128)(2,1)S(1)} %maximum_select_fusion.2), channel_id=1, source_target_pairs={{0,8},{8,0},{16,24},{24,16},{1,9},{9,1},{17,25},{25,17},{2,10},{10... | collective-permute-start | bytes 2064392 | tf_op jit(solution)/shard_map/ppermute | solution.py:44
  45.7 2.0 %copy-start.3 = (bf16[1,512,3584]{2,1,0:T(8,128)(2,1)S(1)}, bf16[1,512,3584]{2,1,0:T(8,128)(2,1)}, u32[]{:S(2)}) copy-start(bf16[1,512,3584]{2,1,0:T(8,128)(2,1)} %param.13) | copy-start | bytes 11010052
  48.7 2.0 %copy-start.2 = (bf16[1,3584,512]{2,1,0:T(8,128)(2,1)S(1)}, bf16[1,3584,512]{2,1,0:T(8,128)(2,1)}, u32[]{:S(2)}) copy-start(bf16[1,3584,512]{2,1,0:T(8,128)(2,1)} %param.12) | copy-start | bytes 11010052
  50.7 2.0 %copy-start.1 = (bf16[1,3584,512]{2,1,0:T(8,128)(2,1)S(1)}, bf16[1,3584,512]{2,1,0:T(8,128)(2,1)}, u32[]{:S(2)}) copy-start(bf16[1,3584,512]{2,1,0:T(8,128)(2,1)} %param.11) | copy-start | bytes 11010052
  54.2 2.9 %copy-start.4 = (bf16[192,512,1]{1,0,2:T(8,128)(2,1)}, bf16[192,512,1]{1,0,2:T(8,128)(2,1)S(1)}, u32[]{:S(2)}) copy-start(bf16[192,512,1]{1,0,2:T(8,128)(2,1)S(1)} %get-tuple-element.29) | copy-start | bytes 589828
  58.6 5.1 %collective-permute-start.8 = (bf16[2,192,896]{2,1,0:T(8,128)(2,1)S(1)}, bf16[2,192,896]{2,1,0:T(8,128)(2,1)S(1)}, u32[]{:S(2)}, u32[]{:S(2)}) collective-permute-start(bf16[2,192,896]{2,1,0:T(8,128)(2,1)S(1)} %fusion.18), channel_id=1, source_target_pairs={{0,8},{8,0},{16,24},{24,16},{1,9},{9,1},{17,25},{25,17},{2,10},{10... | collective-permute-start | bytes 2064392 | tf_op jit(solution)/shard_map/ppermute | solution.py:60
  59.9 4.6 %collective-permute-start.2 = (bf16[2,192,896]{2,1,0:T(8,128)(2,1)S(1)}, bf16[2,192,896]{2,1,0:T(8,128)(2,1)S(1)}, u32[]{:S(2)}, u32[]{:S(2)}) collective-permute-start(bf16[2,192,896]{2,1,0:T(8,128)(2,1)S(1)} %fusion.17), channel_id=1, source_target_pairs={{0,8},{8,0},{16,24},{24,16},{1,9},{9,1},{17,25},{25,17},{2,10},{10... | collective-permute-start | bytes 2064392 | tf_op jit(solution)/shard_map/ppermute | solution.py:60
  60.0 2.1 %collective-permute-start.6 = (f32[192]{0:T(256)S(1)}, f32[192]{0:T(256)S(1)}, u32[]{:S(2)}, u32[]{:S(2)}) collective-permute-start(f32[192]{0:T(256)S(1)} %get-tuple-element.25), channel_id=1, source_target_pairs={{0,8},{8,0},{16,24},{24,16},{1,9},{9,1},{17,25},{25,17},{2,10},{10... | collective-permute-start | bytes 2312 | tf_op jit(solution)/shard_map/ppermute | solution.py:67
  62.2 19.3 %collective-permute-start.7 = (f32[192]{0:T(256)S(1)}, f32[192]{0:T(256)S(1)}, u32[]{:S(2)}, u32[]{:S(2)}) collective-permute-start(f32[192]{0:T(256)S(1)} %add.53), channel_id=1, source_target_pairs={{0,16},{8,24},{16,0},{24,8},{1,17},{9,25},{17,1},{25,9},{2,18},{10... | collective-permute-start | bytes 2312 | tf_op jit(solution)/shard_map/ppermute | solution.py:67
  63.9 11.0 %collective-permute-start.9 = (bf16[1,192,896]{2,1,0:T(8,128)(2,1)S(1)}, bf16[1,192,896]{2,1,0:T(8,128)(2,1)S(1)}, u32[]{:S(2)}, u32[]{:S(2)}) collective-permute-start(bf16[1,192,896]{2,1,0:T(8,128)(2,1)S(1)} %fusion.24), channel_id=1, source_target_pairs={{0,16},{8,24},{16,0},{24,8},{1,17},{9,25},{17,1},{25,9},{2,18},{10... | collective-permute-start | bytes 1032200 | tf_op jit(solution)/shard_map/ppermute | solution.py:60
  65.5 17.7 %collective-permute-start.3 = (bf16[1,192,896]{2,1,0:T(8,128)(2,1)}, bf16[1,192,896]{2,1,0:T(8,128)(2,1)}, u32[]{:S(2)}, u32[]{:S(2)}) collective-permute-start(bf16[1,192,896]{2,1,0:T(8,128)(2,1)} %fusion.23), channel_id=1, source_target_pairs={{0,16},{8,24},{16,0},{24,8},{1,17},{9,25},{17,1},{25,9},{2,18},{10... | collective-permute-start | bytes 1032200 | tf_op jit(solution)/shard_map/ppermute | solution.py:60
  75.8 14.6 %all-to-all-start.3 = ((bf16[8,24,896]{2,1,0:T(8,128)(2,1)}), bf16[8,24,896]{2,1,0:T(8,128)(2,1)S(1)}, u32[]{:S(2)}, u32[]{:S(2)}) async-start(bf16[8,24,896]{2,1,0:T(8,128)(2,1)} %bitcast.185), calls=%async_computation.3 | async-start | bytes 688128 | tf_op jit(solution)/shard_map/all_to_all | solution.py:98
  83.2 1.1 %copy-start.7 = (bf16[8,24,1]{2,1,0:T(8,128)(2,1)S(1)}, bf16[8,24,1]{2,1,0:T(8,128)(2,1)}, u32[]{:S(2)}) copy-start(bf16[8,24,1]{2,1,0:T(8,128)(2,1)} %concatenate.62) | copy-start | bytes 1156
  83.2 1.1 %copy-start.8 = (bf16[8,24,1]{2,1,0:T(8,128)(2,1)S(1)}, bf16[8,24,1]{2,1,0:T(8,128)(2,1)}, u32[]{:S(2)}) copy-start(bf16[8,24,1]{2,1,0:T(8,128)(2,1)} %concatenate.63) | copy-start | bytes 1156
  84.3 9.7 %copy-start.5 = (bf16[192,512,1]{1,0,2:T(8,128)(2,1)S(1)}, bf16[192,512,1]{1,0,2:T(8,128)(2,1)}, u32[]{:S(2)}) copy-start(bf16[192,512,1]{1,0,2:T(8,128)(2,1)} %copy-done.4) | copy-start | bytes 589828
  90.3 13.0 %all-to-all-start.2 = ((bf16[8,24,1024]{2,1,0:T(8,128)(2,1)}), bf16[8,24,1024]{2,1,0:T(8,128)(2,1)S(1)}, u32[]{:S(2)}, u32[]{:S(2)}) async-start(bf16[8,24,1024]{2,1,0:T(8,128)(2,1)} %maximum_maximum_fusion.1), calls=%async_computation.2 | async-start | bytes 786432 | tf_op jit(solution)/shard_map/all_to_all | solution.py:98
  100.0 3.7 %copy-start.9 = (f32[128,1]{0,1:T(1,128)S(1)}, f32[128,1]{0,1:T(1,128)}, u32[]{:S(2)}) copy-start(f32[128,1]{0,1:T(1,128)} %param.10) | copy-start | bytes 1540
where the time goes:
time: 106 us; the launch traced here: 105 us
  waiting for transfers between devices  41.7 us (39%)
  starting transfers between devices  28.1 us (27%)
  matrix products  17.2 us (16%)
  other arithmetic  10.1 us (10%)
  local copies, waits for them, and re-layouts  7.04 us (7%)
    all_to_all x4, starting transfers between devices, to_experts(): got = lax.all_to_all(sent, 'ep', split_axis=0, concat_axis=0, tiled=True)  20.2 us
    all_to_all x4, waiting for transfers between devices, to_experts(): got = lax.all_to_all(sent, 'ep', split_axis=0, concat_axis=0, tiled=True)  17.1 us
    ppermute x4, waiting for transfers between devices, gather_blocks(): other = lax.ppermute(held, 'ctx', xor_pairs(n_ctx, bit))  15 us
    ppermute x4, waiting for transfers between devices, scatter_sum(): got = lax.ppermute(send, 'ctx', xor_pairs(n_ctx, bit))  7.95 us
    unnamed x21, local copies, waits for them, and re-layouts  4.71 us
    ppermute x4, starting transfers between devices, gather_blocks(): other = lax.ppermute(held, 'ctx', xor_pairs(n_ctx, bit))  3.18 us
    dot_general x1, matrix products, shards(): jnp.einsum('nsd,sf->ndf', rows_in, grad_up, preferred_element_type=jnp.fl...  3 us
    dot_general x1, matrix products, shards(): jnp.einsum('nsd,sf->ndf', rows_in, grad_gate, preferred_element_type=jnp....  3 us
  transfers between devices with their start and end apart: 14, of which 8 were waited for; matrix products, arithmetic and copies ran while one was open for 18% of the time, Pallas kernels for 0%

commit v1 on v0

--- a/solution.py
+++ b/solution.py
@@ -2,6 +2,22 @@
 import jax.numpy as jnp
 from jax import lax
 from jax.sharding import PartitionSpec as P
+
+
+def swapped_with_each(x, axis, split, join):
+    ways, here = (lax.axis_size(axis), lax.axis_index(axis))
+    width = x.shape[split] // ways
+    lengths = list(x.shape)
+    lengths[split] = width
+    height = lengths[join]
+    lengths[join] = height * ways
+    full = jnp.zeros(lengths, x.dtype)
+    for mask in range(ways):
+        part = lax.dynamic_slice_in_dim(x, (here ^ mask) * width, width, axis=split)
+        if mask:
+            part = lax.ppermute(part, axis, [(d, d ^ mask) for d in range(ways)])
+        full = lax.dynamic_update_slice_in_dim(full, part, (here ^ mask) * height, axis=join)
+    return full
 
 
 def route_onehot(expert_ids, experts, capacity):
@@ -95,7 +111,7 @@
 
     def to_experts(rows):
         sent = rows.reshape(experts, capacity, rows.shape[1])
-        got = lax.all_to_all(sent, "ep", split_axis=0, concat_axis=0, tiled=True)
+        got = swapped_with_each(sent, "ep", 0, 0)
         return got.reshape(slot_count, rows.shape[1])
 
     slot_gates = jnp.zeros((slot_count,), jnp.float32)

time: 106 us -> 168 us (1.58)
  waiting for transfers between devices: 41.7 us -> 74.7 us
  starting transfers between devices: 28.1 us -> 58.9 us
    ppermute x0 -> x28, starting transfers between devices: none -> 50.9 us  [swapped_with_each(): part = lax.ppermute(part, axis, [(d, d ^ mask) for d in range(ways)])]
    ppermute x0 -> x28, waiting for transfers between devices: none -> 48.3 us  [swapped_with_each(): part = lax.ppermute(part, axis, [(d, d ^ mask) for d in range(ways)])]
    all_to_all x4 -> x0, starting transfers between devices: 20.2 us -> none  [to_experts(): got = lax.all_to_all(sent, 'ep', split_axis=0, concat_axis=0, tiled=True)]
    all_to_all x4 -> x0, waiting for transfers between devices: 17.1 us -> none  [to_experts(): got = lax.all_to_all(sent, 'ep', split_axis=0, concat_axis=0, tiled=True)]
    ppermute x4, waiting for transfers between devices: 7.95 us -> 11.6 us  [scatter_sum(): got = lax.ppermute(send, 'ctx', xor_pairs(n_ctx, bit))]
    reshape x2, other arithmetic: 0.34 us -> 2.76 us  [scatter_sum(): halves = acc.reshape((-1, 2) + acc.shape[1:])]
    unnamed x21 -> x17, local copies, waits for them, and re-layouts: 4.71 us -> 4.7 us
  transfers between devices with their start and end apart: 14 -> 38, of which waited for: 8 -> 20; matrix products, arithmetic and copies ran while one was open for 18% -> 12% of each run, Pallas kernels for 0% -> 0%
where the time goes in v1:
time: 168 us; the launch traced here: 167 us
  waiting for transfers between devices  74.7 us (44%)
  starting transfers between devices  58.9 us (35%)
  matrix products  16.5 us (10%)
  other arithmetic  9.67 us (6%)
  local copies, waits for them, and re-layouts  6.4 us (4%)
    ppermute x28, starting transfers between devices, swapped_with_each(): part = lax.ppermute(part, axis, [(d, d ^ mask) for d in range(ways)])  50.9 us
    ppermute x28, waiting for transfers between devices, swapped_with_each(): part = lax.ppermute(part, axis, [(d, d ^ mask) for d in range(ways)])  48.3 us
    ppermute x4, waiting for transfers between devices, gather_blocks(): other = lax.ppermute(held, 'ctx', xor_pairs(n_ctx, bit))  14.2 us
    ppermute x4, waiting for transfers between devices, scatter_sum(): got = lax.ppermute(send, 'ctx', xor_pairs(n_ctx, bit))  11.6 us
    unnamed x17, local copies, waits for them, and re-layouts  4.7 us
  transfers between devices with their start and end apart: 38, of which 20 were waited for; matrix products, arithmetic and copies ran while one was open for 12% of the time, Pallas kernels for 0%

profile of v1, /device:TPU:0, one launch (start us, length us, event | category | flops | bytes accessed | tf_op | source)
XLA Modules:
  0.0 167.4 jit_solution(9825204864959209741)
XLA Ops:
  2.7 6.0 %collective-permute-start.17 = (bf16[1,24,896]{2,1,0:T(8,128)(2,1)S(1)}, bf16[1,24,896]{2,1,0:T(8,128)(2,1)S(1)}, u32[]{:S(2)}, u32[]{:S(2)}) collective-permute-start(bf16[1,24,896]{2,1,0:T(8,128)(2,1)S(1)} %get-tuple-element.58), channel_id=1, source_target_pairs={{0,7},{1,6},{2,5},{3,4},{4,3},{5,2},{6,1},{7,0},{8,15},{9,14},{10,... | collective-permute-start | bytes 129032 | tf_op jit(solution)/shard_map/ppermute | solution.py:18
  9.7 2.0 %collective-permute-start.14 = (bf16[1,24,896]{2,1,0:T(8,128)(2,1)S(1)}, bf16[1,24,896]{2,1,0:T(8,128)(2,1)S(1)}, u32[]{:S(2)}, u32[]{:S(2)}) collective-permute-start(bf16[1,24,896]{2,1,0:T(8,128)(2,1)S(1)} %get-tuple-element.61), channel_id=1, source_target_pairs={{0,4},{1,5},{2,6},{3,7},{4,0},{5,1},{6,2},{7,3},{8,12},{9,13},{10,... | collective-permute-start | bytes 129032 | tf_op jit(solution)/shard_map/ppermute | solution.py:18
  17.1 3.0 %collective-permute-done.12 = bf16[1,24,896]{2,1,0:T(8,128)(2,1)S(1)} collective-permute-done((bf16[1,24,896]{2,1,0:T(8,128)(2,1)S(1)}, bf16[1,24,896]{2,1,0:T(8,128)(2,1)S(1)}, u32[]{:S(2)}, u32[]{:S(2)}) %collective-permute-start.12) | collective-permute-done | bytes 43040 | tf_op jit(solution)/shard_map/ppermute | solution.py:18
  20.1 2.3 %collective-permute-start.13 = (bf16[1,24,896]{2,1,0:T(8,128)(2,1)S(1)}, bf16[1,24,896]{2,1,0:T(8,128)(2,1)S(1)}, u32[]{:S(2)}, u32[]{:S(2)}) collective-permute-start(bf16[1,24,896]{2,1,0:T(8,128)(2,1)S(1)} %get-tuple-element.62), channel_id=1, source_target_pairs={{0,3},{1,2},{2,1},{3,0},{4,7},{5,6},{6,5},{7,4},{8,11},{9,10},{10,... | collective-permute-start | bytes 129032 | tf_op jit(solution)/shard_map/ppermute | solution.py:18
  22.5 2.6 %collective-permute-done.13 = bf16[1,24,896]{2,1,0:T(8,128)(2,1)S(1)} collective-permute-done((bf16[1,24,896]{2,1,0:T(8,128)(2,1)S(1)}, bf16[1,24,896]{2,1,0:T(8,128)(2,1)S(1)}, u32[]{:S(2)}, u32[]{:S(2)}) %collective-permute-start.13) | collective-permute-done | bytes 43040 | tf_op jit(solution)/shard_map/ppermute | solution.py:18
  25.0 4.6 %collective-permute-start.6 = (bf16[1,24,1024]{2,1,0:T(8,128)(2,1)S(1)}, bf16[1,24,1024]{2,1,0:T(8,128)(2,1)S(1)}, u32[]{:S(2)}, u32[]{:S(2)}) collective-permute-start(bf16[1,24,1024]{2,1,0:T(8,128)(2,1)S(1)} %get-tuple-element.42), channel_id=1, source_target_pairs={{0,7},{1,6},{2,5},{3,4},{4,3},{5,2},{6,1},{7,0},{8,15},{9,14},{10,... | collective-permute-start | bytes 147464 | tf_op jit(solution)/shard_map/ppermute | solution.py:18
  30.8 2.1 %collective-permute-start.3 = (bf16[1,24,1024]{2,1,0:T(8,128)(2,1)S(1)}, bf16[1,24,1024]{2,1,0:T(8,128)(2,1)S(1)}, u32[]{:S(2)}, u32[]{:S(2)}) collective-permute-start(bf16[1,24,1024]{2,1,0:T(8,128)(2,1)S(1)} %get-tuple-element.45), channel_id=1, source_target_pairs={{0,4},{1,5},{2,6},{3,7},{4,0},{5,1},{6,2},{7,3},{8,12},{9,13},{10,... | collective-permute-start | bytes 147464 | tf_op jit(solution)/shard_map/ppermute | solution.py:18
  34.5 2.5 %collective-permute-done = bf16[1,24,1024]{2,1,0:T(8,128)(2,1)S(1)} collective-permute-done((bf16[1,24,1024]{2,1,0:T(8,128)(2,1)S(1)}, bf16[1,24,1024]{2,1,0:T(8,128)(2,1)S(1)}, u32[]{:S(2)}, u32[]{:S(2)}) %collective-permute-start) | collective-permute-done | bytes 49184 | tf_op jit(solution)/shard_map/ppermute | solution.py:18
  38.5 2.7 %collective-permute-done.1 = bf16[1,24,1024]{2,1,0:T(8,128)(2,1)S(1)} collective-permute-done((bf16[1,24,1024]{2,1,0:T(8,128)(2,1)S(1)}, bf16[1,24,1024]{2,1,0:T(8,128)(2,1)S(1)}, u32[]{:S(2)}, u32[]{:S(2)}) %collective-permute-start.1) | collective-permute-done | bytes 49184 | tf_op jit(solution)/shard_map/ppermute | solution.py:18
  41.2 2.3 %collective-permute-start.2 = (bf16[1,24,1024]{2,1,0:T(8,128)(2,1)S(1)}, bf16[1,24,1024]{2,1,0:T(8,128)(2,1)S(1)}, u32[]{:S(2)}, u32[]{:S(2)}) collective-permute-start(bf16[1,24,1024]{2,1,0:T(8,128)(2,1)S(1)} %get-tuple-element.46), channel_id=1, source_target_pairs={{0,3},{1,2},{2,1},{3,0},{4,7},{5,6},{6,5},{7,4},{8,11},{9,10},{10,... | collective-permute-start | bytes 147464 | tf_op jit(solution)/shard_map/ppermute | solution.py:18
  43.5 2.7 %collective-permute-done.2 = bf16[1,24,1024]{2,1,0:T(8,128)(2,1)S(1)} collective-permute-done((bf16[1,24,1024]{2,1,0:T(8,128)(2,1)S(1)}, bf16[1,24,1024]{2,1,0:T(8,128)(2,1)S(1)}, u32[]{:S(2)}, u32[]{:S(2)}) %collective-permute-start.2) | collective-permute-done | bytes 49184 | tf_op jit(solution)/shard_map/ppermute | solution.py:18
  47.8 5.6 %collective-permute-done.18 = bf16[1,192,896]{2,1,0:T(8,128)(2,1)S(1)} collective-permute-done((bf16[1,192,896]{2,1,0:T(8,128)(2,1)S(1)}, bf16[1,192,896]{2,1,0:T(8,128)(2,1)S(1)}, u32[]{:S(2)}, u32[]{:S(2)}) %collective-permute-start.18) | collective-permute-done | bytes 344096 | tf_op jit(solution)/shard_map/ppermute | solution.py:60
  56.4 8.6 %collective-permute-done.7 = bf16[1,192,896]{2,1,0:T(8,128)(2,1)S(1)} collective-permute-done((bf16[1,192,896]{2,1,0:T(8,128)(2,1)S(1)}, bf16[1,192,896]{2,1,0:T(8,128)(2,1)S(1)}, u32[]{:S(2)}, u32[]{:S(2)}) %collective-permute-start.7) | collective-permute-done | bytes 344096 | tf_op jit(solution)/shard_map/ppermute | solution.py:60
  77.7 3.0 %convolution_convert_fusion = bf16[4,896,512]{2,1,0:T(8,128)(2,1)} fusion(bf16[4,192,896]{2,1,0:T(8,128)(2,1)S(1)} %bitcast.160, bf16[192,512,1]{1,0,2:T(8,128)(2,1)S(1)} %get-tuple-element.29), kind=kOutput, calls=%fused_computation.4 | convolution fusion | flops 706478080 | bytes 5242880 | tf_op jit(solution)/shard_map/nsd,sf->ndf/dot_general | solution.py:172
  83.1 3.0 %convolution_convert_fusion.1 = bf16[4,896,512]{2,1,0:T(8,128)(2,1)} fusion(bf16[4,192,896]{2,1,0:T(8,128)(2,1)S(1)} %bitcast.161, bf16[192,512]{1,0:T(8,128)(2,1)S(1)} %get-tuple-element.30), kind=kOutput, calls=%fused_computation.5 | convolution fusion | flops 706478080 | bytes 5242880 | tf_op jit(solution)/shard_map/nsd,sf->ndf/dot_general | solution.py:167
  95.5 7.5 %collective-permute-done.30 = bf16[1,192,896]{2,1,0:T(8,128)(2,1)S(1)} collective-permute-done((bf16[1,192,896]{2,1,0:T(8,128)(2,1)S(1)}, bf16[1,192,896]{2,1,0:T(8,128)(2,1)S(1)}, u32[]{:S(2)}, u32[]{:S(2)}) %collective-permute-start.30) | collective-permute-done | bytes 344096 | tf_op jit(solution)/shard_map/ppermute | solution.py:76
  104.8 4.1 %collective-permute-done.10 = bf16[1,192,896]{2,1,0:T(8,128)(2,1)S(1)} collective-permute-done((bf16[1,192,896]{2,1,0:T(8,128)(2,1)S(1)}, bf16[1,192,896]{2,1,0:T(8,128)(2,1)S(1)}, u32[]{:S(2)}, u32[]{:S(2)}) %collective-permute-start.10) | collective-permute-done | bytes 344096 | tf_op jit(solution)/shard_map/ppermute | solution.py:76
  109.2 5.2 %collective-permute-start.28 = (bf16[1,24,1024]{2,1,0:T(8,128)(2,1)S(1)}, bf16[1,24,1024]{2,1,0:T(8,128)(2,1)S(1)}, u32[]{:S(2)}, u32[]{:S(2)}) collective-permute-start(bf16[1,24,1024]{2,1,0:T(8,128)(2,1)S(1)} %get-tuple-element.32), channel_id=1, source_target_pairs={{0,7},{1,6},{2,5},{3,4},{4,3},{5,2},{6,1},{7,0},{8,15},{9,14},{10,... | collective-permute-start | bytes 147464 | tf_op jit(solution)/shard_map/ppermute | solution.py:18
  114.9 2.4 %collective-permute-start.25 = (bf16[1,24,1024]{2,1,0:T(8,128)(2,1)S(1)}, bf16[1,24,1024]{2,1,0:T(8,128)(2,1)S(1)}, u32[]{:S(2)}, u32[]{:S(2)}) collective-permute-start(bf16[1,24,1024]{2,1,0:T(8,128)(2,1)S(1)} %get-tuple-element.35), channel_id=1, source_target_pairs={{0,4},{1,5},{2,6},{3,7},{4,0},{5,1},{6,2},{7,3},{8,12},{9,13},{10,... | collective-permute-start | bytes 147464 | tf_op jit(solution)/shard_map/ppermute | solution.py:18
  118.8 3.2 %collective-permute-done.32 = bf16[1,24,896]{2,1,0:T(8,128)(2,1)S(1)} collective-permute-done((bf16[1,24,896]{2,1,0:T(8,128)(2,1)S(1)}, bf16[1,24,896]{2,1,0:T(8,128)(2,1)S(1)}, u32[]{:S(2)}, u32[]{:S(2)}) %collective-permute-start.32) | collective-permute-done | bytes 43040 | tf_op jit(solution)/shard_map/ppermute | solution.py:18
  123.8 3.0 %collective-permute-done.33 = bf16[1,24,896]{2,1,0:T(8,128)(2,1)S(1)} collective-permute-done((bf16[1,24,896]{2,1,0:T(8,128)(2,1)S(1)}, bf16[1,24,896]{2,1,0:T(8,128)(2,1)S(1)}, u32[]{:S(2)}, u32[]{:S(2)}) %collective-permute-start.33) | collective-permute-done | bytes 43040 | tf_op jit(solution)/shard_map/ppermute | solution.py:18
  126.9 2.2 %collective-permute-start.34 = (bf16[1,24,896]{2,1,0:T(8,128)(2,1)S(1)}, bf16[1,24,896]{2,1,0:T(8,128)(2,1)S(1)}, u32[]{:S(2)}, u32[]{:S(2)}) collective-permute-start(bf16[1,24,896]{2,1,0:T(8,128)(2,1)S(1)} %get-tuple-element.53), channel_id=1, source_target_pairs={{0,4},{1,5},{2,6},{3,7},{4,0},{5,1},{6,2},{7,3},{8,12},{9,13},{10,... | collective-permute-start | bytes 129032 | tf_op jit(solution)/shard_map/ppermute | solution.py:18
  129.1 3.9 %collective-permute-done.34 = bf16[1,24,896]{2,1,0:T(8,128)(2,1)S(1)} collective-permute-done((bf16[1,24,896]{2,1,0:T(8,128)(2,1)S(1)}, bf16[1,24,896]{2,1,0:T(8,128)(2,1)S(1)}, u32[]{:S(2)}, u32[]{:S(2)}) %collective-permute-start.34) | collective-permute-done | bytes 43040 | tf_op jit(solution)/shard_map/ppermute | solution.py:18
  133.1 2.5 %collective-permute-start.35 = (bf16[1,24,896]{2,1,0:T(8,128)(2,1)S(1)}, bf16[1,24,896]{2,1,0:T(8,128)(2,1)S(1)}, u32[]{:S(2)}, u32[]{:S(2)}) collective-permute-start(bf16[1,24,896]{2,1,0:T(8,128)(2,1)S(1)} %get-tuple-element.52), channel_id=1, source_target_pairs={{0,5},{1,4},{2,7},{3,6},{4,1},{5,0},{6,3},{7,2},{8,13},{9,12},{10,... | collective-permute-start | bytes 129032 | tf_op jit(solution)/shard_map/ppermute | solution.py:18
  135.5 4.3 %collective-permute-done.35 = bf16[1,24,896]{2,1,0:T(8,128)(2,1)S(1)} collective-permute-done((bf16[1,24,896]{2,1,0:T(8,128)(2,1)S(1)}, bf16[1,24,896]{2,1,0:T(8,128)(2,1)S(1)}, u32[]{:S(2)}, u32[]{:S(2)}) %collective-permute-start.35) | collective-permute-done | bytes 43040 | tf_op jit(solution)/shard_map/ppermute | solution.py:18
  139.8 2.5 %collective-permute-start.36 = (bf16[1,24,896]{2,1,0:T(8,128)(2,1)S(1)}, bf16[1,24,896]{2,1,0:T(8,128)(2,1)S(1)}, u32[]{:S(2)}, u32[]{:S(2)}) collective-permute-start(bf16[1,24,896]{2,1,0:T(8,128)(2,1)S(1)} %get-tuple-element.51), channel_id=1, source_target_pairs={{0,6},{1,7},{2,4},{3,5},{4,2},{5,3},{6,0},{7,1},{8,14},{9,15},{10,... | collective-permute-start | bytes 129032 | tf_op jit(solution)/shard_map/ppermute | solution.py:18
  142.3 3.3 %collective-permute-done.36 = bf16[1,24,896]{2,1,0:T(8,128)(2,1)S(1)} collective-permute-done((bf16[1,24,896]{2,1,0:T(8,128)(2,1)S(1)}, bf16[1,24,896]{2,1,0:T(8,128)(2,1)S(1)}, u32[]{:S(2)}, u32[]{:S(2)}) %collective-permute-start.36) | collective-permute-done | bytes 43040 | tf_op jit(solution)/shard_map/ppermute | solution.py:18
  145.6 3.1 %collective-permute-start.37 = (bf16[1,24,896]{2,1,0:T(8,128)(2,1)S(1)}, bf16[1,24,896]{2,1,0:T(8,128)(2,1)S(1)}, u32[]{:S(2)}, u32[]{:S(2)}) collective-permute-start(bf16[1,24,896]{2,1,0:T(8,128)(2,1)S(1)} %get-tuple-element.50), channel_id=1, source_target_pairs={{0,7},{1,6},{2,5},{3,4},{4,3},{5,2},{6,1},{7,0},{8,15},{9,14},{10,... | collective-permute-start | bytes 129032 | tf_op jit(solution)/shard_map/ppermute | solution.py:18
  148.7 3.6 %collective-permute-done.37 = bf16[1,24,896]{2,1,0:T(8,128)(2,1)S(1)} collective-permute-done((bf16[1,24,896]{2,1,0:T(8,128)(2,1)S(1)}, bf16[1,24,896]{2,1,0:T(8,128)(2,1)S(1)}, u32[]{:S(2)}, u32[]{:S(2)}) %collective-permute-start.37) | collective-permute-done | bytes 43040 | tf_op jit(solution)/shard_map/ppermute | solution.py:18
  153.8 2.7 %collective-permute-done.22 = bf16[1,24,1024]{2,1,0:T(8,128)(2,1)S(1)} collective-permute-done((bf16[1,24,1024]{2,1,0:T(8,128)(2,1)S(1)}, bf16[1,24,1024]{2,1,0:T(8,128)(2,1)S(1)}, u32[]{:S(2)}, u32[]{:S(2)}) %collective-permute-start.22) | collective-permute-done | bytes 49184 | tf_op jit(solution)/shard_map/ppermute | solution.py:18
  156.5 4.1 %collective-permute-done.23 = bf16[1,24,1024]{2,1,0:T(8,128)(2,1)S(1)} collective-permute-done((bf16[1,24,1024]{2,1,0:T(8,128)(2,1)S(1)}, bf16[1,24,1024]{2,1,0:T(8,128)(2,1)S(1)}, u32[]{:S(2)}, u32[]{:S(2)}) %collective-permute-start.23) | collective-permute-done | bytes 49184 | tf_op jit(solution)/shard_map/ppermute | solution.py:18
  160.6 5.0 %collective-permute-done.24 = bf16[1,24,1024]{2,1,0:T(8,128)(2,1)S(1)} collective-permute-done((bf16[1,24,1024]{2,1,0:T(8,128)(2,1)S(1)}, bf16[1,24,1024]{2,1,0:T(8,128)(2,1)S(1)}, u32[]{:S(2)}, u32[]{:S(2)}) %collective-permute-start.24) | collective-permute-done | bytes 49184 | tf_op jit(solution)/shard_map/ppermute | solution.py:18
  (151 shorter events, 50.6 us)
Async XLA Ops:
  2.7 30.3 %collective-permute-start.17 = (bf16[1,24,896]{2,1,0:T(8,128)(2,1)S(1)}, bf16[1,24,896]{2,1,0:T(8,128)(2,1)S(1)}, u32[]{:S(2)}, u32[]{:S(2)}) collective-permute-start(bf16[1,24,896]{2,1,0:T(8,128)(2,1)S(1)} %get-tuple-element.58), channel_id=1, source_target_pairs={{0,7},{1,6},{2,5},{3,4},{4,3},{5,2},{6,1},{7,0},{8,15},{9,14},{10,... | collective-permute-start | bytes 129032 | tf_op jit(solution)/shard_map/ppermute | solution.py:18
  8.7 22.1 %collective-permute-start.16 = (bf16[1,24,896]{2,1,0:T(8,128)(2,1)S(1)}, bf16[1,24,896]{2,1,0:T(8,128)(2,1)S(1)}, u32[]{:S(2)}, u32[]{:S(2)}) collective-permute-start(bf16[1,24,896]{2,1,0:T(8,128)(2,1)S(1)} %get-tuple-element.59), channel_id=1, source_target_pairs={{0,6},{1,7},{2,4},{3,5},{4,2},{5,3},{6,0},{7,1},{8,14},{9,15},{10,... | collective-permute-start | bytes 129032 | tf_op jit(solution)/shard_map/ppermute | solution.py:18
  8.9 21.0 %collective-permute-start.15 = (bf16[1,24,896]{2,1,0:T(8,128)(2,1)S(1)}, bf16[1,24,896]{2,1,0:T(8,128)(2,1)S(1)}, u32[]{:S(2)}, u32[]{:S(2)}) collective-permute-start(bf16[1,24,896]{2,1,0:T(8,128)(2,1)S(1)} %get-tuple-element.60), channel_id=1, source_target_pairs={{0,5},{1,4},{2,7},{3,6},{4,1},{5,0},{6,3},{7,2},{8,13},{9,12},{10,... | collective-permute-start | bytes 129032 | tf_op jit(solution)/shard_map/ppermute | solution.py:18
  9.7 20.0 %collective-permute-start.14 = (bf16[1,24,896]{2,1,0:T(8,128)(2,1)S(1)}, bf16[1,24,896]{2,1,0:T(8,128)(2,1)S(1)}, u32[]{:S(2)}, u32[]{:S(2)}) collective-permute-start(bf16[1,24,896]{2,1,0:T(8,128)(2,1)S(1)} %get-tuple-element.61), channel_id=1, source_target_pairs={{0,4},{1,5},{2,6},{3,7},{4,0},{5,1},{6,2},{7,3},{8,12},{9,13},{10,... | collective-permute-start | bytes 129032 | tf_op jit(solution)/shard_map/ppermute | solution.py:18
  11.7 4.4 %collective-permute-start.11 = (bf16[1,24,896]{2,1,0:T(8,128)(2,1)S(1)}, bf16[1,24,896]{2,1,0:T(8,128)(2,1)S(1)}, u32[]{:S(2)}, u32[]{:S(2)}) collective-permute-start(bf16[1,24,896]{2,1,0:T(8,128)(2,1)S(1)} %get-tuple-element.64), channel_id=1, source_target_pairs={{0,1},{1,0},{2,3},{3,2},{4,5},{5,4},{6,7},{7,6},{8,9},{9,8},{10,11... | collective-permute-start | bytes 129032 | tf_op jit(solution)/shard_map/ppermute | solution.py:18
  20.1 4.9 %collective-permute-start.13 = (bf16[1,24,896]{2,1,0:T(8,128)(2,1)S(1)}, bf16[1,24,896]{2,1,0:T(8,128)(2,1)S(1)}, u32[]{:S(2)}, u32[]{:S(2)}) collective-permute-start(bf16[1,24,896]{2,1,0:T(8,128)(2,1)S(1)} %get-tuple-element.62), channel_id=1, source_target_pairs={{0,3},{1,2},{2,1},{3,0},{4,7},{5,6},{6,5},{7,4},{8,11},{9,10},{10,... | collective-permute-start | bytes 129032 | tf_op jit(solution)/shard_map/ppermute | solution.py:18
  25.0 22.8 %collective-permute-start.6 = (bf16[1,24,1024]{2,1,0:T(8,128)(2,1)S(1)}, bf16[1,24,1024]{2,1,0:T(8,128)(2,1)S(1)}, u32[]{:S(2)}, u32[]{:S(2)}) collective-permute-start(bf16[1,24,1024]{2,1,0:T(8,128)(2,1)S(1)} %get-tuple-element.42), channel_id=1, source_target_pairs={{0,7},{1,6},{2,5},{3,4},{4,3},{5,2},{6,1},{7,0},{8,15},{9,14},{10,... | collective-permute-start | bytes 147464 | tf_op jit(solution)/shard_map/ppermute | solution.py:18
  29.6 18.1 %collective-permute-start.5 = (bf16[1,24,1024]{2,1,0:T(8,128)(2,1)S(1)}, bf16[1,24,1024]{2,1,0:T(8,128)(2,1)S(1)}, u32[]{:S(2)}, u32[]{:S(2)}) collective-permute-start(bf16[1,24,1024]{2,1,0:T(8,128)(2,1)S(1)} %get-tuple-element.43), channel_id=1, source_target_pairs={{0,6},{1,7},{2,4},{3,5},{4,2},{5,3},{6,0},{7,1},{8,14},{9,15},{10,... | collective-permute-start | bytes 147464 | tf_op jit(solution)/shard_map/ppermute | solution.py:18
  29.9 17.8 %collective-permute-start.4 = (bf16[1,24,1024]{2,1,0:T(8,128)(2,1)S(1)}, bf16[1,24,1024]{2,1,0:T(8,128)(2,1)S(1)}, u32[]{:S(2)}, u32[]{:S(2)}) collective-permute-start(bf16[1,24,1024]{2,1,0:T(8,128)(2,1)S(1)} %get-tuple-element.44), channel_id=1, source_target_pairs={{0,5},{1,4},{2,7},{3,6},{4,1},{5,0},{6,3},{7,2},{8,13},{9,12},{10,... | collective-permute-start | bytes 147464 | tf_op jit(solution)/shard_map/ppermute | solution.py:18
  30.8 16.9 %collective-permute-start.3 = (bf16[1,24,1024]{2,1,0:T(8,128)(2,1)S(1)}, bf16[1,24,1024]{2,1,0:T(8,128)(2,1)S(1)}, u32[]{:S(2)}, u32[]{:S(2)}) collective-permute-start(bf16[1,24,1024]{2,1,0:T(8,128)(2,1)S(1)} %get-tuple-element.45), channel_id=1, source_target_pairs={{0,4},{1,5},{2,6},{3,7},{4,0},{5,1},{6,2},{7,3},{8,12},{9,13},{10,... | collective-permute-start | bytes 147464 | tf_op jit(solution)/shard_map/ppermute | solution.py:18
  32.9 4.2 %collective-permute-start = (bf16[1,24,1024]{2,1,0:T(8,128)(2,1)S(1)}, bf16[1,24,1024]{2,1,0:T(8,128)(2,1)S(1)}, u32[]{:S(2)}, u32[]{:S(2)}) collective-permute-start(bf16[1,24,1024]{2,1,0:T(8,128)(2,1)S(1)} %get-tuple-element.48), channel_id=1, source_target_pairs={{0,1},{1,0},{2,3},{3,2},{4,5},{5,4},{6,7},{7,6},{8,9},{9,8},{10,11... | collective-permute-start | bytes 147464 | tf_op jit(solution)/shard_map/ppermute | solution.py:18
  41.2 5.0 %collective-permute-start.2 = (bf16[1,24,1024]{2,1,0:T(8,128)(2,1)S(1)}, bf16[1,24,1024]{2,1,0:T(8,128)(2,1)S(1)}, u32[]{:S(2)}, u32[]{:S(2)}) collective-permute-start(bf16[1,24,1024]{2,1,0:T(8,128)(2,1)S(1)} %get-tuple-element.46), channel_id=1, source_target_pairs={{0,3},{1,2},{2,1},{3,0},{4,7},{5,6},{6,5},{7,4},{8,11},{9,10},{10,... | collective-permute-start | bytes 147464 | tf_op jit(solution)/shard_map/ppermute | solution.py:18
  46.1 7.2 %collective-permute-start.18 = (bf16[1,192,896]{2,1,0:T(8,128)(2,1)S(1)}, bf16[1,192,896]{2,1,0:T(8,128)(2,1)S(1)}, u32[]{:S(2)}, u32[]{:S(2)}) collective-permute-start(bf16[1,192,896]{2,1,0:T(8,128)(2,1)S(1)} %bitcast.174), channel_id=1, source_target_pairs={{0,16},{8,24},{16,0},{24,8},{1,17},{9,25},{17,1},{25,9},{2,18},{10... | collective-permute-start | bytes 1032200 | tf_op jit(solution)/shard_map/ppermute | solution.py:60
  54.4 10.9 %collective-permute-start.19 = (bf16[2,192,896]{2,1,0:T(8,128)(2,1)}, bf16[2,192,896]{2,1,0:T(8,128)(2,1)S(1)}, u32[]{:S(2)}, u32[]{:S(2)}) collective-permute-start(bf16[2,192,896]{2,1,0:T(8,128)(2,1)} %maximum_select_fusion.4), channel_id=1, source_target_pairs={{0,8},{8,0},{16,24},{24,16},{1,9},{9,1},{17,25},{25,17},{2,10},{10... | collective-permute-start | bytes 2064392 | tf_op jit(solution)/shard_map/ppermute | solution.py:60
  54.4 10.5 %collective-permute-start.7 = (bf16[1,192,896]{2,1,0:T(8,128)(2,1)S(1)}, bf16[1,192,896]{2,1,0:T(8,128)(2,1)S(1)}, u32[]{:S(2)}, u32[]{:S(2)}) collective-permute-start(bf16[1,192,896]{2,1,0:T(8,128)(2,1)S(1)} %get-tuple-element.41), channel_id=1, source_target_pairs={{0,16},{8,24},{16,0},{24,8},{1,17},{9,25},{17,1},{25,9},{2,18},{10... | collective-permute-start | bytes 1032200 | tf_op jit(solution)/shard_map/ppermute | solution.py:60
  75.8 10.4 %collective-permute-start.20 = (f32[192]{0:T(256)S(1)}, f32[192]{0:T(256)S(1)}, u32[]{:S(2)}, u32[]{:S(2)}) collective-permute-start(f32[192]{0:T(256)S(1)} %get-tuple-element.25), channel_id=1, source_target_pairs={{0,8},{8,0},{16,24},{24,16},{1,9},{9,1},{17,25},{25,17},{2,10},{10... | collective-permute-start | bytes 2312 | tf_op jit(solution)/shard_map/ppermute | solution.py:83
  83.1 7.4 %collective-permute-start.29 = (bf16[2,192,896]{2,1,0:T(8,128)(2,1)}, bf16[2,192,896]{2,1,0:T(8,128)(2,1)}, u32[]{:S(2)}, u32[]{:S(2)}) collective-permute-start(bf16[2,192,896]{2,1,0:T(8,128)(2,1)} %fusion.18), channel_id=1, source_target_pairs={{0,8},{8,0},{16,24},{24,16},{1,9},{9,1},{17,25},{25,17},{2,10},{10... | collective-permute-start | bytes 2064392 | tf_op jit(solution)/shard_map/ppermute | solution.py:76
  89.0 4.6 %collective-permute-start.9 = (bf16[2,192,896]{2,1,0:T(8,128)(2,1)}, bf16[2,192,896]{2,1,0:T(8,128)(2,1)}, u32[]{:S(2)}, u32[]{:S(2)}) collective-permute-start(bf16[2,192,896]{2,1,0:T(8,128)(2,1)} %fusion.17), channel_id=1, source_target_pairs={{0,8},{8,0},{16,24},{24,16},{1,9},{9,1},{17,25},{25,17},{2,10},{10... | collective-permute-start | bytes 2064392 | tf_op jit(solution)/shard_map/ppermute | solution.py:76
  91.9 11.1 %collective-permute-start.30 = (bf16[1,192,896]{2,1,0:T(8,128)(2,1)S(1)}, bf16[1,192,896]{2,1,0:T(8,128)(2,1)S(1)}, u32[]{:S(2)}, u32[]{:S(2)}) collective-permute-start(bf16[1,192,896]{2,1,0:T(8,128)(2,1)S(1)} %fusion.24), channel_id=1, source_target_pairs={{0,16},{8,24},{16,0},{24,8},{1,17},{9,25},{17,1},{25,9},{2,18},{10... | collective-permute-start | bytes 1032200 | tf_op jit(solution)/shard_map/ppermute | solution.py:76
  95.0 13.9 %collective-permute-start.10 = (bf16[1,192,896]{2,1,0:T(8,128)(2,1)S(1)}, bf16[1,192,896]{2,1,0:T(8,128)(2,1)S(1)}, u32[]{:S(2)}, u32[]{:S(2)}) collective-permute-start(bf16[1,192,896]{2,1,0:T(8,128)(2,1)S(1)} %fusion.23), channel_id=1, source_target_pairs={{0,16},{8,24},{16,0},{24,8},{1,17},{9,25},{17,1},{25,9},{2,18},{10... | collective-permute-start | bytes 1032200 | tf_op jit(solution)/shard_map/ppermute | solution.py:76
  103.2 14.2 %collective-permute-start.31 = (bf16[1,24,896]{2,1,0:T(8,128)(2,1)S(1)}, bf16[1,24,896]{2,1,0:T(8,128)(2,1)S(1)}, u32[]{:S(2)}, u32[]{:S(2)}) collective-permute-start(bf16[1,24,896]{2,1,0:T(8,128)(2,1)S(1)} %get-tuple-element.56), channel_id=1, source_target_pairs={{0,1},{1,0},{2,3},{3,2},{4,5},{5,4},{6,7},{7,6},{8,9},{9,8},{10,11... | collective-permute-start | bytes 129032 | tf_op jit(solution)/shard_map/ppermute | solution.py:18
  109.2 56.4 %collective-permute-start.28 = (bf16[1,24,1024]{2,1,0:T(8,128)(2,1)S(1)}, bf16[1,24,1024]{2,1,0:T(8,128)(2,1)S(1)}, u32[]{:S(2)}, u32[]{:S(2)}) collective-permute-start(bf16[1,24,1024]{2,1,0:T(8,128)(2,1)S(1)} %get-tuple-element.32), channel_id=1, source_target_pairs={{0,7},{1,6},{2,5},{3,4},{4,3},{5,2},{6,1},{7,0},{8,15},{9,14},{10,... | collective-permute-start | bytes 147464 | tf_op jit(solution)/shard_map/ppermute | solution.py:18
  114.4 51.2 %collective-permute-start.27 = (bf16[1,24,1024]{2,1,0:T(8,128)(2,1)S(1)}, bf16[1,24,1024]{2,1,0:T(8,128)(2,1)S(1)}, u32[]{:S(2)}, u32[]{:S(2)}) collective-permute-start(bf16[1,24,1024]{2,1,0:T(8,128)(2,1)S(1)} %get-tuple-element.33), channel_id=1, source_target_pairs={{0,6},{1,7},{2,4},{3,5},{4,2},{5,3},{6,0},{7,1},{8,14},{9,15},{10,... | collective-permute-start | bytes 147464 | tf_op jit(solution)/shard_map/ppermute | solution.py:18
  114.4 51.2 %collective-permute-start.26 = (bf16[1,24,1024]{2,1,0:T(8,128)(2,1)S(1)}, bf16[1,24,1024]{2,1,0:T(8,128)(2,1)S(1)}, u32[]{:S(2)}, u32[]{:S(2)}) collective-permute-start(bf16[1,24,1024]{2,1,0:T(8,128)(2,1)S(1)} %get-tuple-element.34), channel_id=1, source_target_pairs={{0,5},{1,4},{2,7},{3,6},{4,1},{5,0},{6,3},{7,2},{8,13},{9,12},{10,... | collective-permute-start | bytes 147464 | tf_op jit(solution)/shard_map/ppermute | solution.py:18
  114.9 50.6 %collective-permute-start.25 = (bf16[1,24,1024]{2,1,0:T(8,128)(2,1)S(1)}, bf16[1,24,1024]{2,1,0:T(8,128)(2,1)S(1)}, u32[]{:S(2)}, u32[]{:S(2)}) collective-permute-start(bf16[1,24,1024]{2,1,0:T(8,128)(2,1)S(1)} %get-tuple-element.35), channel_id=1, source_target_pairs={{0,4},{1,5},{2,6},{3,7},{4,0},{5,1},{6,2},{7,3},{8,12},{9,13},{10,... | collective-permute-start | bytes 147464 | tf_op jit(solution)/shard_map/ppermute | solution.py:18
  117.4 4.6 %collective-permute-start.32 = (bf16[1,24,896]{2,1,0:T(8,128)(2,1)S(1)}, bf16[1,24,896]{2,1,0:T(8,128)(2,1)S(1)}, u32[]{:S(2)}, u32[]{:S(2)}) collective-permute-start(bf16[1,24,896]{2,1,0:T(8,128)(2,1)S(1)} %get-tuple-element.55), channel_id=1, source_target_pairs={{0,2},{1,3},{2,0},{3,1},{4,6},{5,7},{6,4},{7,5},{8,10},{9,11},{10,... | collective-permute-start | bytes 129032 | tf_op jit(solution)/shard_map/ppermute | solution.py:18
  122.0 4.9 %collective-permute-start.33 = (bf16[1,24,896]{2,1,0:T(8,128)(2,1)S(1)}, bf16[1,24,896]{2,1,0:T(8,128)(2,1)S(1)}, u32[]{:S(2)}, u32[]{:S(2)}) collective-permute-start(bf16[1,24,896]{2,1,0:T(8,128)(2,1)S(1)} %get-tuple-element.54), channel_id=1, source_target_pairs={{0,3},{1,2},{2,1},{3,0},{4,7},{5,6},{6,5},{7,4},{8,11},{9,10},{10,... | collective-permute-start | bytes 129032 | tf_op jit(solution)/shard_map/ppermute | solution.py:18
  126.9 6.2 %collective-permute-start.34 = (bf16[1,24,896]{2,1,0:T(8,128)(2,1)S(1)}, bf16[1,24,896]{2,1,0:T(8,128)(2,1)S(1)}, u32[]{:S(2)}, u32[]{:S(2)}) collective-permute-start(bf16[1,24,896]{2,1,0:T(8,128)(2,1)S(1)} %get-tuple-element.53), channel_id=1, source_target_pairs={{0,4},{1,5},{2,6},{3,7},{4,0},{5,1},{6,2},{7,3},{8,12},{9,13},{10,... | collective-permute-start | bytes 129032 | tf_op jit(solution)/shard_map/ppermute | solution.py:18
  133.1 6.8 %collective-permute-start.35 = (bf16[1,24,896]{2,1,0:T(8,128)(2,1)S(1)}, bf16[1,24,896]{2,1,0:T(8,128)(2,1)S(1)}, u32[]{:S(2)}, u32[]{:S(2)}) collective-permute-start(bf16[1,24,896]{2,1,0:T(8,128)(2,1)S(1)} %get-tuple-element.52), channel_id=1, source_target_pairs={{0,5},{1,4},{2,7},{3,6},{4,1},{5,0},{6,3},{7,2},{8,13},{9,12},{10,... | collective-permute-start | bytes 129032 | tf_op jit(solution)/shard_map/ppermute | solution.py:18
  139.8 5.8 %collective-permute-start.36 = (bf16[1,24,896]{2,1,0:T(8,128)(2,1)S(1)}, bf16[1,24,896]{2,1,0:T(8,128)(2,1)S(1)}, u32[]{:S(2)}, u32[]{:S(2)}) collective-permute-start(bf16[1,24,896]{2,1,0:T(8,128)(2,1)S(1)} %get-tuple-element.51), channel_id=1, source_target_pairs={{0,6},{1,7},{2,4},{3,5},{4,2},{5,3},{6,0},{7,1},{8,14},{9,15},{10,... | collective-permute-start | bytes 129032 | tf_op jit(solution)/shard_map/ppermute | solution.py:18
  145.6 6.7 %collective-permute-start.37 = (bf16[1,24,896]{2,1,0:T(8,128)(2,1)S(1)}, bf16[1,24,896]{2,1,0:T(8,128)(2,1)S(1)}, u32[]{:S(2)}, u32[]{:S(2)}) collective-permute-start(bf16[1,24,896]{2,1,0:T(8,128)(2,1)S(1)} %get-tuple-element.50), channel_id=1, source_target_pairs={{0,7},{1,6},{2,5},{3,4},{4,3},{5,2},{6,1},{7,0},{8,15},{9,14},{10,... | collective-permute-start | bytes 129032 | tf_op jit(solution)/shard_map/ppermute | solution.py:18
  160.5 5.0 %collective-permute-start.24 = (bf16[1,24,1024]{2,1,0:T(8,128)(2,1)S(1)}, bf16[1,24,1024]{2,1,0:T(8,128)(2,1)S(1)}, u32[]{:S(2)}, u32[]{:S(2)}) collective-permute-start(bf16[1,24,1024]{2,1,0:T(8,128)(2,1)S(1)} %get-tuple-element.36), channel_id=1, source_target_pairs={{0,3},{1,2},{2,1},{3,0},{4,7},{5,6},{6,5},{7,4},{8,11},{9,10},{10,... | collective-permute-start | bytes 147464 | tf_op jit(solution)/shard_map/ppermute | solution.py:18
  (14 other events, 62.0 us)
